TPU v7x, 32 devices: a whole 2x2x4 slice. The times are simulated.
32 devices in a mesh: grp: 2 (over y), row: 4 (over z), col: 2 (over x), sub: 2 (over core).
Axes of the slice: x: 2, y: 2, z: 4, core: 2. Of those that a mesh axis runs over, the one named last changes fastest.
Arguments:
- a_blocks: bfloat16 [16, 2, 4, 2, 256, 256], P(('grp', 'row', 'sub'), 'col'), parts along dimension 0, may hold values from 20 to 2000
- block_list: int32 [16, 2, 4, 2], P(('grp', 'row', 'sub'), 'col'), parts along dimension 0, may hold values from 0 to 3, as said below
- block_count: int32 [16, 2, 4], P(('grp', 'row', 'sub'), 'col'), parts along dimension 0, may hold values from 1 to 2
- w_factor: bfloat16 [16, 1024, 256], P(('grp', 'row', 'sub')), parts along dimension 0, may hold values from 0.05 to 4
- h_factor: bfloat16 [256, 4096], P(None, ('grp', 'row', 'col')), parts along dimension 1, may hold values from 0.05 to 4
Outputs:
- w_new: float32 [16, 1024, 256], P(('grp', 'row', 'sub'), 'col'), parts along dimension 0
- h_new: float32 [256, 4096], P(None, ('grp', 'row', 'col')), parts along dimension 1
There are 2 independent parts, one for each index of `grp`. A program takes and returns all parts, laid end to end along the dimension named above; each array names one. Nothing has to cross between parts.
Inputs may be any that keep to these rules, and one draw needn't show every extreme that they name: `block_list`: within one block row and column group the 2 slots name different column blocks.
All inputs are finite; a program needn't handle non-finite values.
Results may differ from a plain program's by a relative error of at most 0.0003.
Values may be sent and summed in bfloat16 or wider, within the bound.
No kernel may reach another device: no remote copies, remote signals or barrier semaphores. Data moves between devices by JAX's collectives and lax.ppermute only.
A program may use at most 64 MiB of HBM per device.

v0:
```python
import jax
import jax.numpy as jnp
from jax import lax
from jax.sharding import PartitionSpec as P


def body(a_blocks, block_list, block_count, w_factor, h_factor):
    values = a_blocks[0, 0]
    lists = block_list[0, 0]
    counts = block_count[0, 0]
    w_tile = w_factor[0]
    row_blocks, stored, width = (values.shape[0], values.shape[1], values.shape[2])
    rank = w_tile.shape[1]
    tile_rows = w_tile.shape[0]
    n_row = lax.axis_size("row")
    w_rows = w_tile.reshape(row_blocks, width, rank)
    h_all = lax.all_gather(h_factor, "row", axis=1, tiled=True)
    numer_h = jnp.zeros((rank, n_row * width), jnp.float32)
    parts_w = []
    for brow in range(row_blocks):
        part_w = jnp.zeros((width, rank), jnp.float32)
        for slot in range(stored):
            target = lists[brow, slot]
            live = slot < counts[brow]
            h_block = lax.dynamic_slice_in_dim(h_all, target * width, width, 1)
            product = jnp.dot(w_rows[brow], h_block, preferred_element_type=jnp.float32)
            ratios = (values[brow, slot].astype(jnp.float32) / product).astype(jnp.bfloat16)
            ratios = jnp.where(live, ratios, jnp.zeros_like(ratios))
            part_h = jnp.einsum(
                "ik,ij->kj", w_rows[brow], ratios, preferred_element_type=jnp.float32
            )
            part_w = part_w + jnp.einsum(
                "ij,kj->ik", ratios, h_block, preferred_element_type=jnp.float32
            )
            old = lax.dynamic_slice_in_dim(numer_h, target * width, width, 1)
            numer_h = lax.dynamic_update_slice_in_dim(numer_h, old + part_h, target * width, 1)
        parts_w.append(part_w)
    numer_w = jnp.stack(parts_w).reshape(tile_rows, rank)
    col_first = lax.axis_index("col") == 0
    sub_first = lax.axis_index("sub") == 0
    w_sum = jnp.sum(w_tile.astype(jnp.float32), axis=0)
    h_sum = jnp.sum(h_factor.astype(jnp.float32), axis=1)
    sums = jnp.concatenate([jnp.where(col_first, w_sum, 0.0), jnp.where(sub_first, h_sum, 0.0)])
    sums = lax.psum(sums, ("row", "col", "sub"))
    w_total = sums[:rank]
    h_total = sums[rank:]
    numer_h = lax.psum_scatter(numer_h, "row", scatter_dimension=1, tiled=True)
    numer_h = lax.psum(numer_h, "sub")
    h_new = h_factor.astype(jnp.float32) * numer_h / w_total[:, None]
    share = tile_rows // lax.axis_size("col")
    col_index = lax.axis_index("col")
    mine = lax.psum_scatter(numer_w, "col", scatter_dimension=0, tiled=True)
    w_part = lax.dynamic_slice_in_dim(w_tile, col_index * share, share, 0).astype(jnp.float32)
    w_new = (w_part * mine / h_total[None, :])[None]
    return (w_new, h_new)


def solution(mesh):
    placed = (
        P(("grp", "row", "sub"), "col", None, None, None, None),
        P(("grp", "row", "sub"), "col", None, None),
        P(("grp", "row", "sub"), "col", None),
        P(("grp", "row", "sub"), None, None),
        P(None, ("grp", "row", "col")),
    )
    return jax.shard_map(
        body,
        mesh=mesh,
        in_specs=placed,
        out_specs=(P(("grp", "row", "sub"), "col", None), P(None, ("grp", "row", "col"))),
        check_vma=False,
    )
```

profile of v0, /device:TPU:0, one launch (start us, length us, event | category | flops | bytes accessed | tf_op | source)
XLA Modules:
  0.0 123.8 jit_solution(1494217705936552093)
XLA Ops:
  7.2 1.5 %fusion.116 = (s32[1,1,1]{2,1,0:T(1,128)}, s32[1,1,1]{2,1,0:T(1,128)}, s32[1,1,1]{2,1,0:T(1,128)}, s32[1,1,1]{2,1,0:T(1,128)}) fusion(s32[1,1,4]{2,1,0:T(1,128)} %param.7), kind=kLoop, calls=%fused_computation.152 | loop fusion | bytes 32 | tf_op jit(solution)/shard_map/slice | solution.py:24
  13.8 0.7 copy-done.3
  14.5 0.7 fusion.115
  20.1 17.6 %all_gather.3 = bf16[256,1024]{1,0:T(8,128)(2,1)S(1)} all-gather(bf16[256,256]{1,0:T(8,128)(2,1)} %param.9), channel_id=1, replica_groups=mesh['grp'=2,'row'=4,'col'=2,'sub'=2] {'row'}, dimensions={1}, use_global_device_ids=true | all-gather | bytes 655360 | tf_op jit(solution)/shard_map/all_gather | solution.py:17
  37.7 1.5 %copy.7 = bf16[1,1,4,2,256,256]{4,5,3,2,1,0:T(8,128)(2,1)S(1)} copy(bf16[1,1,4,2,256,256]{5,4,3,2,1,0:T(8,128)(2,1)} %param.5) | data formatting | bytes 2097152 | tf_op args[0]
  39.3 0.3 fusion.35
  39.5 0.3 fusion.36
  39.8 0.2 fusion.37
  40.0 0.2 fusion.38
  40.3 0.3 fusion.39
  40.6 0.2 fusion.40
  40.8 0.3 fusion.41
  41.1 0.2 fusion.42
  41.6 0.2 fusion.17
  42.4 0.2 fusion.9
  43.0 1.0 copy-done
  44.1 0.2 fusion.79
  44.3 0.2 fusion.3
  44.6 0.2 fusion.74
  44.8 0.2 fusion.2
  45.1 0.2 fusion.69
  45.3 0.2 fusion.1
  45.5 0.2 fusion.64
  45.8 0.2 fusion
  46.0 1.1 pad_maximum_fusion
  47.1 0.8 copy-done.2
  48.3 30.9 %psum.14 = f32[512]{0:T(512)S(1)} all-reduce(f32[512]{0:T(512)S(1)} %pad_maximum_fusion.1), channel_id=1, replica_groups=mesh['grp'=2,'row'=4,'col'=2,'sub'=2] {'row','col','sub'}, use_global_device_ids=true, to_apply=%region_3.4 | all-reduce | flops 512 | bytes 4096 | tf_op jit(solution)/shard_map/psum | solution.py:44
  79.3 15.5 %reduce-scatter.3.cloned.1.call-done = f32[512,256]{1,0:T(8,128)} async-done(((f32[1024,256]{1,0:T(8,128)}), f32[512,256]{1,0:T(8,128)}) %reduce-scatter.3.cloned.1.call-update) | async-done | bytes 524304 | tf_op jit(solution)/shard_map/reduce_scatter | solution.py:52
  94.8 1.9 %fusion.44 = f32[1,512,256]{2,1,0:T(8,128)} fusion(f32[512,256]{1,0:T(8,128)} %reduce-scatter.3.cloned.1.call-done, f32[256]{0:T(256)S(1)} %get-tuple-element.5, bf16[1,1024,256]{2,1,0:T(8,128)(2,1)S(1)} %copy-done.1, s32[]{:T(128)S(6)} %select_n.106), kind=kLoop, calls=%fused_computation.67 | loop fusion | flops 393216 | bytes 1311748 | tf_op jit(solution)/shard_map/broadcast_in_dim | solution.py:54
  96.7 18.7 %all-reduce.2.cloned.1.call-done = f32[256,256]{0,1:T(8,128)} async-done(((f32[256,256]{0,1:T(8,128)}), f32[256,256]{0,1:T(8,128)}) %all-reduce.2.cloned.1.call-update) | async-done | bytes 262160 | tf_op jit(solution)/shard_map/psum | solution.py:48
  115.4 1.0 fusion.45
  116.4 0.8 copy.9
  (26 shorter events, 1.7 us)
Async XLA Ops:
  7.2 72.1 %reduce-scatter.5.cloned.1.call-start = ((), (), s32[]{:S(2)}) async-start(), calls=%async_computation.3 | async-start | bytes 1310720 | tf_op jit(solution)/shard_map/reduce_scatter | solution.py:47
  13.8 0.7 copy-start.3
  37.7 1.6 %copy-start.1 = (bf16[1,1024,256]{2,1,0:T(8,128)(2,1)S(1)}, bf16[1,1024,256]{2,1,0:T(8,128)(2,1)}, u32[]{:S(2)}) copy-start(bf16[1,1024,256]{2,1,0:T(8,128)(2,1)} %param.8) | copy-start | bytes 1572868
  43.0 1.0 copy-start
  44.1 50.7 %reduce-scatter.3.cloned.1.call-start = ((), (), s32[]{:S(2)}) async-start(), calls=%async_computation.2 | async-start | bytes 1572864 | tf_op jit(solution)/shard_map/reduce_scatter | solution.py:52
  47.1 0.9 copy-start.2
  47.1 68.3 %all-reduce.2.cloned.1.call-start = ((), (), s32[]{:S(2)}) async-start(), calls=%async_computation.4 | async-start | bytes 524288 | tf_op jit(solution)/shard_map/psum | solution.py:48
Sparse Core Ops, SparseCore 0:
  44.2 29.1 reduce-scatter.4
  75.7 18.9 reduce-scatter.2
  97.1 18.2 all-reduce.1
where the time goes:
time: 124 us
  blocking collectives  48.5 us (39%)
  waiting for transfers between devices  34.3 us (28%)
  between operations  24.2 us (20%)
  local copies, waits for them, and re-layouts  7.19 us (6%)
  matrix products  5.36 us (4%)
  other arithmetic  4.15 us (3%)
    psum x1, blocking collectives, body(): sums = lax.psum(sums, ('row', 'col', 'sub'))  30.9 us
    psum x1, waiting for transfers between devices, body(): numer_h = lax.psum(numer_h, 'sub')  18.7 us
    all_gather x1, blocking collectives, body(): h_all = lax.all_gather(h_factor, 'row', axis=1, tiled=True)  17.6 us
    reduce_scatter x1, waiting for transfers between devices, body(): mine = lax.psum_scatter(numer_w, 'col', scatter_dimension=0, tiled=True)  15.5 us
    unnamed x11, local copies, waits for them, and re-layouts  5 us
  transfers between devices with their start and end apart: 3, of which 2 were waited for; matrix products, arithmetic and copies ran while one was open for 4% of the time, Pallas kernels for 0%

commit v1 on v0

--- a/solution.py
+++ b/solution.py
@@ -45,7 +45,7 @@
     w_total = sums[:rank]
     h_total = sums[rank:]
     numer_h = lax.psum_scatter(numer_h, "row", scatter_dimension=1, tiled=True)
-    numer_h = lax.psum(numer_h, "sub")
+    numer_h = jnp.sum(lax.all_gather(numer_h, "sub"), axis=0)
     h_new = h_factor.astype(jnp.float32) * numer_h / w_total[:, None]
     share = tile_rows // lax.axis_size("col")
     col_index = lax.axis_index("col")

time: 124 us -> 104 us (0.84)
  waiting for transfers between devices: 34.3 us -> 11.3 us
  blocking collectives: 48.5 us -> 50.9 us
    psum x1 -> x0, waiting for transfers between devices: 18.7 us -> none  [body(): numer_h = lax.psum(numer_h, 'sub')]
    reduce_scatter x1, waiting for transfers between devices: 15.5 us -> 11.2 us  [body(): mine = lax.psum_scatter(numer_w, 'col', scatter_dimension=0, tiled=True)]
    all_gather x0 -> x1, blocking collectives: none -> 2.39 us  [body(): numer_h = jnp.sum(lax.all_gather(numer_h, 'sub'), axis=0)]
  transfers between devices with their start and end apart: 3 -> 2, of which waited for: 2 -> 1; matrix products, arithmetic and copies ran while one was open for 4% -> 5% of each run, Pallas kernels for 0% -> 0%
where the time goes in v1:
time: 104 us; the launch traced here: 103 us
  blocking collectives  50.9 us (49%)
  between operations  24.5 us (24%)
  waiting for transfers between devices  11.3 us (11%)
  local copies, waits for them, and re-layouts  7.58 us (7%)
  matrix products  5.36 us (5%)
  other arithmetic  3.85 us (4%)
    psum x1, blocking collectives, body(): sums = lax.psum(sums, ('row', 'col', 'sub'))  30.9 us
    all_gather x1, blocking collectives, body(): h_all = lax.all_gather(h_factor, 'row', axis=1, tiled=True)  17.6 us
    reduce_scatter x1, waiting for transfers between devices, body(): mine = lax.psum_scatter(numer_w, 'col', scatter_dimension=0, tiled=True)  11.2 us
    unnamed x11, local copies, waits for them, and re-layouts  5.04 us
    all_gather x1, blocking collectives, body(): numer_h = jnp.sum(lax.all_gather(numer_h, 'sub'), axis=0)  2.39 us
  transfers between devices with their start and end apart: 2, of which 1 were waited for; matrix products, arithmetic and copies ran while one was open for 5% of the time, Pallas kernels for 0%

profile of v1, /device:TPU:0, one launch (start us, length us, event | category | flops | bytes accessed | tf_op | source)
XLA Modules:
  0.0 103.5 jit_solution(2542642004216063831)
XLA Ops:
  7.2 1.5 %fusion.116 = (s32[1,1,1]{2,1,0:T(1,128)}, s32[1,1,1]{2,1,0:T(1,128)}, s32[1,1,1]{2,1,0:T(1,128)}, s32[1,1,1]{2,1,0:T(1,128)}) fusion(s32[1,1,4]{2,1,0:T(1,128)} %param.7), kind=kLoop, calls=%fused_computation.152 | loop fusion | bytes 32 | tf_op jit(solution)/shard_map/slice | solution.py:24
  13.8 0.7 copy-done.3
  14.5 0.7 fusion.115
  20.1 17.6 %all_gather.9 = bf16[256,1024]{1,0:T(8,128)(2,1)S(1)} all-gather(bf16[256,256]{1,0:T(8,128)(2,1)} %param.9), channel_id=1, replica_groups=mesh['grp'=2,'row'=4,'col'=2,'sub'=2] {'row'}, dimensions={1}, use_global_device_ids=true | all-gather | bytes 655360 | tf_op jit(solution)/shard_map/all_gather | solution.py:17
  37.7 1.5 %copy.8 = bf16[1,1,4,2,256,256]{4,5,3,2,1,0:T(8,128)(2,1)S(1)} copy(bf16[1,1,4,2,256,256]{5,4,3,2,1,0:T(8,128)(2,1)} %param.5) | data formatting | bytes 2097152 | tf_op args[0]
  39.3 0.3 fusion.35
  39.5 0.3 fusion.36
  39.8 0.2 fusion.37
  40.0 0.2 fusion.38
  40.3 0.3 fusion.39
  40.6 0.2 fusion.40
  40.8 0.3 fusion.41
  41.1 0.2 fusion.42
  42.4 0.2 fusion.9
  43.0 1.0 copy-done
  44.1 0.2 fusion.79
  44.3 0.2 fusion.3
  44.6 0.2 fusion.74
  44.8 0.2 fusion.2
  45.1 0.2 fusion.69
  45.3 0.2 fusion.1
  45.5 0.2 fusion.64
  45.8 0.2 fusion
  46.0 1.1 %pad_maximum_fusion = f32[4,256,256]{2,1,0:T(8,128)} fusion(f32[1,256,256]{2,1,0:T(8,128)S(1)} %fusion, f32[1,256,256]{2,1,0:T(8,128)S(1)} %fusion.1, f32[1,256,256]{2,1,0:T(8,128)S(1)} %fusion.2, f32[1,256,256]{2,1,0:T(8,128)S(1)} %fusion.3), kind=kLoop, calls=%fused_computation.63 | loop fusion | flops 786432 | bytes 2097152 | tf_op jit(solution)/shard_map/stack | solution.py:38
  47.1 0.9 copy-done.2
  48.4 30.9 %psum.7 = f32[512]{0:T(512)S(1)} all-reduce(f32[512]{0:T(512)S(1)} %pad_maximum_fusion.1), channel_id=1, replica_groups=mesh['grp'=2,'row'=4,'col'=2,'sub'=2] {'row','col','sub'}, use_global_device_ids=true, to_apply=%region_3.4 | all-reduce | flops 512 | bytes 4096 | tf_op jit(solution)/shard_map/psum | solution.py:44
  79.3 2.4 %all-gather = f32[512,256]{0,1:T(8,128)S(1)} all-gather(f32[256,256]{0,1:T(8,128)} %reduce-scatter.5.cloned.1.call-done), channel_id=2, replica_groups=mesh['grp'=2,'row'=4,'col'=2,'sub'=2] {'sub'}, dimensions={0}, use_global_device_ids=true | all-gather | bytes 786432 | tf_op jit(solution)/shard_map/all_gather | solution.py:48
  81.7 0.3 reshape.87
  82.0 0.6 reduce_sum.29
  82.7 0.8 copy.10
  83.5 11.2 %reduce-scatter.3.cloned.1.call-done = f32[512,256]{1,0:T(8,128)} async-done(((f32[1024,256]{1,0:T(8,128)}), f32[512,256]{1,0:T(8,128)}) %reduce-scatter.3.cloned.1.call-update) | async-done | bytes 524304 | tf_op jit(solution)/shard_map/reduce_scatter | solution.py:52
  94.8 1.9 %fusion.44 = f32[1,512,256]{2,1,0:T(8,128)} fusion(f32[512,256]{1,0:T(8,128)} %reduce-scatter.3.cloned.1.call-done, f32[256]{0:T(256)S(1)} %get-tuple-element.5, bf16[1,1024,256]{2,1,0:T(8,128)(2,1)S(1)} %copy-done.1, s32[]{:T(128)S(6)} %select_n.106), kind=kLoop, calls=%fused_computation.67 | loop fusion | flops 393216 | bytes 1311748 | tf_op jit(solution)/shard_map/broadcast_in_dim | solution.py:54
  (26 shorter events, 1.9 us)
Async XLA Ops:
  7.2 72.1 %reduce-scatter.5.cloned.1.call-start = ((), (), s32[]{:S(2)}) async-start(), calls=%async_computation.3 | async-start | bytes 1310720 | tf_op jit(solution)/shard_map/reduce_scatter | solution.py:47
  13.8 0.7 copy-start.3
  37.7 1.6 %copy-start.1 = (bf16[1,1024,256]{2,1,0:T(8,128)(2,1)S(1)}, bf16[1,1024,256]{2,1,0:T(8,128)(2,1)}, u32[]{:S(2)}) copy-start(bf16[1,1024,256]{2,1,0:T(8,128)(2,1)} %param.8) | copy-start | bytes 1572868
  43.0 1.0 copy-start
  44.1 50.7 %reduce-scatter.3.cloned.1.call-start = ((), (), s32[]{:S(2)}) async-start(), calls=%async_computation.2 | async-start | bytes 1572864 | tf_op jit(solution)/shard_map/reduce_scatter | solution.py:52
  47.1 0.9 copy-start.2
Sparse Core Ops, SparseCore 0:
  44.2 29.1 reduce-scatter.4
  75.7 18.9 reduce-scatter.2

commit v2 on v0

--- a/solution.py
+++ b/solution.py
@@ -14,7 +14,16 @@
     tile_rows = w_tile.shape[0]
     n_row = lax.axis_size("row")
     w_rows = w_tile.reshape(row_blocks, width, rank)
-    h_all = lax.all_gather(h_factor, "row", axis=1, tiled=True)
+    ways = lax.axis_size("row")
+    up = [(d, (d + 1) % ways) for d in range(ways)]
+    down = [(d, (d - 1) % ways) for d in range(ways)]
+    earlier, later = ([h_factor], [h_factor])
+    for _ in range(ways // 2):
+        earlier.append(lax.ppermute(earlier[-1], "row", up))
+    for _ in range((ways - 1) // 2):
+        later.append(lax.ppermute(later[-1], "row", down))
+    line = jnp.concatenate([*earlier[::-1], *later[1:]], axis=1)
+    h_all = jnp.roll(line, (lax.axis_index("row") - ways // 2) * h_factor.shape[1], axis=1)
     numer_h = jnp.zeros((rank, n_row * width), jnp.float32)
     parts_w = []
     for brow in range(row_blocks):

time: 124 us -> 119 us (0.960)
  blocking collectives: 48.5 us -> 32.3 us
  starting transfers between devices: 0.12 us -> 5.29 us
  local copies, waits for them, and re-layouts: 7.19 us -> 9.44 us
  waiting for transfers between devices: 34.3 us -> 36.4 us
  matrix products: 5.36 us -> 6.65 us
    all_gather x1 -> x0, blocking collectives: 17.6 us -> none  [body(): h_all = lax.all_gather(h_factor, 'row', axis=1, tiled=True)]
    ppermute x0 -> x3, starting transfers between devices: none -> 5.17 us  [the longest x2 3.08 us: body(): earlier.append(lax.ppermute(earlier[-1], 'row', up))]
    ppermute x0 -> x3, waiting for transfers between devices: none -> 4.48 us  [the longest x2 4.48 us: body(): earlier.append(lax.ppermute(earlier[-1], 'row', up))]
    reduce_scatter x1, waiting for transfers between devices: 15.5 us -> 13.1 us  [body(): mine = lax.psum_scatter(numer_w, 'col', scatter_dimension=0, tiled=True)]
    unnamed x11 -> x26, local copies, waits for them, and re-layouts: 5 us -> 7.21 us
    psum x1, blocking collectives: 30.9 us -> 32.3 us  [body(): sums = lax.psum(sums, ('row', 'col', 'sub'))]
  transfers between devices with their start and end apart: 3 -> 6, of which waited for: 2 -> 3; matrix products, arithmetic and copies ran while one was open for 4% -> 8% of each run, Pallas kernels for 0% -> 0%
where the time goes in v2:
time: 119 us
  waiting for transfers between devices  36.4 us (31%)
  blocking collectives  32.3 us (27%)
  between operations  24.4 us (21%)
  local copies, waits for them, and re-layouts  9.44 us (8%)
  matrix products  6.65 us (6%)
  starting transfers between devices  5.29 us (4%)
  other arithmetic  4.14 us (3%)
    psum x1, blocking collectives, body(): sums = lax.psum(sums, ('row', 'col', 'sub'))  32.3 us
    psum x1, waiting for transfers between devices, body(): numer_h = lax.psum(numer_h, 'sub')  18.7 us
    reduce_scatter x1, waiting for transfers between devices, body(): mine = lax.psum_scatter(numer_w, 'col', scatter_dimension=0, tiled=True)  13.1 us
    unnamed x26, local copies, waits for them, and re-layouts  7.21 us
    ppermute x2, waiting for transfers between devices, body(): earlier.append(lax.ppermute(earlier[-1], 'row', up))  4.48 us
    ppermute x2, starting transfers between devices, body(): earlier.append(lax.ppermute(earlier[-1], 'row', up))  3.08 us
    dot_general x8, matrix products, body(): product = jnp.dot(w_rows[brow], h_block, preferred_element_type=jnp.float32)  2.68 us
    dot_general x8, matrix products, body(): jnp.einsum('ij,kj->ik', ratios, h_block, preferred_element_type=jnp.float32)  2.44 us
  transfers between devices with their start and end apart: 6, of which 3 were waited for; matrix products, arithmetic and copies ran while one was open for 8% of the time, Pallas kernels for 0%

profile of v2, /device:TPU:0, one launch (start us, length us, event | category | flops | bytes accessed | tf_op | source)
XLA Modules:
  0.0 118.6 jit_solution(9403272897273784533)
XLA Ops:
  7.2 3.1 %collective-permute-start = (bf16[256,256]{1,0:T(8,128)(2,1)}, bf16[256,256]{1,0:T(8,128)(2,1)S(1)}, u32[]{:S(2)}, u32[]{:S(2)}) collective-permute-start(bf16[256,256]{1,0:T(8,128)(2,1)} %param.9), channel_id=1, source_target_pairs={{0,4},{4,8},{8,12},{12,0},{1,5},{5,9},{9,13},{13,1},{2,6},{6,10},{... | collective-permute-start | bytes 393224 | tf_op jit(solution)/shard_map/ppermute | solution.py:22
  10.3 2.1 %collective-permute-start.2 = (bf16[256,256]{1,0:T(8,128)(2,1)}, bf16[256,256]{1,0:T(8,128)(2,1)S(1)}, u32[]{:S(2)}, u32[]{:S(2)}) collective-permute-start(bf16[256,256]{1,0:T(8,128)(2,1)} %param.9), channel_id=1, source_target_pairs={{0,12},{4,0},{8,4},{12,8},{1,13},{5,1},{9,5},{13,9},{2,14},{6,2},{... | collective-permute-start | bytes 393224 | tf_op jit(solution)/shard_map/ppermute | solution.py:24
  12.4 4.5 %collective-permute-done = bf16[256,256]{1,0:T(8,128)(2,1)S(1)} collective-permute-done((bf16[256,256]{1,0:T(8,128)(2,1)}, bf16[256,256]{1,0:T(8,128)(2,1)S(1)}, u32[]{:S(2)}, u32[]{:S(2)}) %collective-permute-start) | collective-permute-done | bytes 131104 | tf_op jit(solution)/shard_map/ppermute | solution.py:22
  16.9 1.5 %fusion.116 = (s32[1,1,1]{2,1,0:T(1,128)}, s32[1,1,1]{2,1,0:T(1,128)}, s32[1,1,1]{2,1,0:T(1,128)}, s32[1,1,1]{2,1,0:T(1,128)}) fusion(s32[1,1,4]{2,1,0:T(1,128)} %param.7), kind=kLoop, calls=%fused_computation.160 | loop fusion | bytes 32 | tf_op jit(solution)/shard_map/slice | solution.py:33
  23.4 0.7 copy-done.7
  24.1 0.7 fusion.115
  29.9 1.5 %copy.7 = bf16[1,1,4,2,256,256]{4,5,3,2,1,0:T(8,128)(2,1)S(1)} copy(bf16[1,1,4,2,256,256]{5,4,3,2,1,0:T(8,128)(2,1)} %param.5) | data formatting | bytes 2097152 | tf_op args[0]
  31.4 0.9 copy-done.2
  32.4 1.0 copy-done.1
  33.4 0.3 fusion.35
  33.7 0.3 fusion.36
  34.1 0.3 fusion.37
  34.4 0.3 fusion.38
  34.8 0.3 fusion.39
  35.1 0.3 fusion.40
  35.5 0.3 fusion.41
  35.8 0.3 fusion.42
  37.9 1.0 copy-done
  39.0 0.3 fusion.77
  39.3 0.3 fusion.3
  39.6 0.3 fusion.72
  39.9 0.6 copy-done.6
  41.1 0.6 copy-done.4
  42.0 0.3 fusion.62
  42.3 0.3 fusion
  42.6 1.0 pad_maximum_fusion
  44.1 32.3 %psum.14 = f32[512]{0:T(512)S(1)} all-reduce(f32[512]{0:T(512)S(1)} %pad_maximum_fusion.1), channel_id=1, replica_groups=mesh['grp'=2,'row'=4,'col'=2,'sub'=2] {'row','col','sub'}, use_global_device_ids=true, to_apply=%region_3.4 | all-reduce | flops 512 | bytes 4096 | tf_op jit(solution)/shard_map/psum | solution.py:53
  76.5 13.1 %reduce-scatter.3.cloned.1.call-done = f32[512,256]{1,0:T(8,128)} async-done(((f32[1024,256]{1,0:T(8,128)}), f32[512,256]{1,0:T(8,128)}) %reduce-scatter.3.cloned.1.call-update) | async-done | bytes 524304 | tf_op jit(solution)/shard_map/reduce_scatter | solution.py:61
  89.6 1.9 %fusion.44 = f32[1,512,256]{2,1,0:T(8,128)} fusion(f32[512,256]{1,0:T(8,128)} %reduce-scatter.3.cloned.1.call-done, f32[256]{0:T(256)S(1)} %get-tuple-element.5, bf16[1,1024,256]{2,1,0:T(8,128)(2,1)S(1)} %copy-done.1, s32[]{:T(128)S(6)} %select_n.137), kind=kLoop, calls=%fused_computation.67 | loop fusion | flops 393216 | bytes 1311748 | tf_op jit(solution)/shard_map/broadcast_in_dim | solution.py:63
  91.5 18.7 %all-reduce.2.cloned.1.call-done = f32[256,256]{0,1:T(8,128)} async-done(((f32[256,256]{0,1:T(8,128)}), f32[256,256]{0,1:T(8,128)}) %all-reduce.2.cloned.1.call-update) | async-done | bytes 262160 | tf_op jit(solution)/shard_map/psum | solution.py:57
  110.2 1.0 fusion.45
  111.2 0.8 copy.9
  (47 shorter events, 3.1 us)
Async XLA Ops:
  7.2 69.3 %reduce-scatter.5.cloned.1.call-start = ((), (), s32[]{:S(2)}) async-start(), calls=%async_computation.3 | async-start | bytes 1310720 | tf_op jit(solution)/shard_map/reduce_scatter | solution.py:56
  7.2 9.6 %collective-permute-start = (bf16[256,256]{1,0:T(8,128)(2,1)}, bf16[256,256]{1,0:T(8,128)(2,1)S(1)}, u32[]{:S(2)}, u32[]{:S(2)}) collective-permute-start(bf16[256,256]{1,0:T(8,128)(2,1)} %param.9), channel_id=1, source_target_pairs={{0,4},{4,8},{8,12},{12,0},{1,5},{5,9},{9,13},{13,1},{2,6},{6,10},{... | collective-permute-start | bytes 393224 | tf_op jit(solution)/shard_map/ppermute | solution.py:22
  10.3 22.0 %collective-permute-start.2 = (bf16[256,256]{1,0:T(8,128)(2,1)}, bf16[256,256]{1,0:T(8,128)(2,1)S(1)}, u32[]{:S(2)}, u32[]{:S(2)}) collective-permute-start(bf16[256,256]{1,0:T(8,128)(2,1)} %param.9), channel_id=1, source_target_pairs={{0,12},{4,0},{8,4},{12,8},{1,13},{5,1},{9,5},{13,9},{2,14},{6,2},{... | collective-permute-start | bytes 393224 | tf_op jit(solution)/shard_map/ppermute | solution.py:24
  16.9 14.5 %collective-permute-start.1 = (bf16[256,256]{1,0:T(8,128)(2,1)S(1)}, bf16[256,256]{1,0:T(8,128)(2,1)S(1)}, u32[]{:S(2)}, u32[]{:S(2)}) collective-permute-start(bf16[256,256]{1,0:T(8,128)(2,1)S(1)} %collective-permute-done), channel_id=1, source_target_pairs={{0,4},{4,8},{8,12},{12,0},{1,5},{5,9},{9,13},{13,1},{2,6},{6,10},{... | collective-permute-start | bytes 393224 | tf_op jit(solution)/shard_map/ppermute | solution.py:22
  23.4 0.7 copy-start.7
  31.4 0.9 copy-start.2
  32.4 1.0 copy-start.1
  34.8 2.3 %copy-start.3 = (bf16[256,256]{0,1:T(8,128)(2,1)}, bf16[256,256]{0,1:T(8,128)(2,1)S(1)}, u32[]{:S(2)}) copy-start(bf16[256,256]{0,1:T(8,128)(2,1)S(1)} %fusion.38) | copy-start | bytes 393220
  35.5 1.2 copy-start.5
  37.9 1.0 copy-start
  38.9 50.7 %reduce-scatter.3.cloned.1.call-start = ((), (), s32[]{:S(2)}) async-start(), calls=%async_computation.2 | async-start | bytes 1572864 | tf_op jit(solution)/shard_map/reduce_scatter | solution.py:61
  39.6 0.9 copy-start.6
  40.8 0.9 copy-start.4
  43.7 66.5 %all-reduce.2.cloned.1.call-start = ((), (), s32[]{:S(2)}) async-start(), calls=%async_computation.4 | async-start | bytes 524288 | tf_op jit(solution)/shard_map/psum | solution.py:57
Sparse Core Ops, SparseCore 0:
  39.0 29.1 reduce-scatter.4
  70.5 19.0 reduce-scatter.2
  91.9 18.2 all-reduce.1
